TPU v7x, 512 devices: a whole 4x8x8 slice. The times are simulated.
512 devices in a mesh: dp: 16 (over x, y_hi, core), ctx: 32 (over z, y_lo).
Axes of the slice: x: 4, y: 8 (y_hi: 2, y_lo: 4; y = y_hi * 4 + y_lo), z: 8, core: 2. Of those that a mesh axis runs over, the one named last changes fastest.
Arguments:
- queries: bfloat16 [16, 4096, 512], P('dp', 'ctx'), may hold values from -6 to 6
- keys: bfloat16 [16, 4096, 512], P('dp', 'ctx'), may hold values from -6 to 6
- values: bfloat16 [16, 4096, 512], P('dp', 'ctx'), may hold values from -6 to 6
- grad_out: bfloat16 [16, 4096, 8192], P('dp', 'ctx'), may hold values from -6 to 6
- out_weight: bfloat16 [512, 8192], P(None, 'ctx'), may hold values from -0.25 to 0.25
- residues: float32 [512, 16], P('ctx'), may hold values from -0.125 to 0.125
- decays: float32 [512, 16], P('ctx'), may hold values from 1.2207031e-05 to 0.1
Outputs:
- grad_queries: bfloat16 [16, 4096, 512], P('dp', None, 'ctx')
- grad_keys: bfloat16 [16, 4096, 512], P('dp', None, 'ctx')
- grad_values: bfloat16 [16, 4096, 512], P('dp', None, 'ctx')
- grad_weight: float32 [512, 8192], P(None, 'ctx')
- grad_residues: float32 [512, 16], P('ctx')
- grad_decays: float32 [512, 16], P('ctx')
All inputs are finite; a program needn't handle non-finite values.
Results may differ from a plain program's by a relative error of at most 0.017.
Values may be sent and summed in bfloat16 or wider, within the bound.
No kernel may reach another device: no remote copies, remote signals or barrier semaphores. Data moves between devices by JAX's collectives and lax.ppermute only.
A program may use at most 128 MiB of HBM per device.

v0:
```python
import math
import jax
import jax.numpy as jnp
from jax import lax
from jax.sharding import PartitionSpec as P

FFT_COLS = 128
HIGHEST = lax.Precision.HIGHEST


def fourier_tables(fft_rows, fft_cols):
    total = fft_rows * fft_cols
    row_index = jnp.arange(fft_rows, dtype=jnp.int32)
    col_index = jnp.arange(fft_cols, dtype=jnp.int32)
    first = (row_index[:, None] * row_index[None, :] % fft_rows).astype(jnp.float32) * (
        2.0 * math.pi / fft_rows
    )
    twist = (row_index[:, None] * col_index[None, :] % total).astype(jnp.float32) * (
        2.0 * math.pi / total
    )
    second = (col_index[:, None] * col_index[None, :] % fft_cols).astype(jnp.float32) * (
        2.0 * math.pi / fft_cols
    )
    return (
        (jnp.cos(first), -jnp.sin(first)),
        (jnp.cos(twist), -jnp.sin(twist)),
        (jnp.cos(second), -jnp.sin(second)),
    )


def complex_product(left_re, left_im, right_re, right_im):
    return (left_re * right_re - left_im * right_im, left_re * right_im + left_im * right_re)


def apply_middle(table_re, table_im, data_re):

    def single(table, data):
        return jnp.einsum("kn,cnm->ckm", table, data, precision=HIGHEST)

    return (single(table_re, data_re), single(table_im, data_re))


def apply_last(table_re, table_im, data_re, data_im):

    def single(data, table):
        return jnp.einsum("ckm,mj->ckj", data, table, precision=HIGHEST)

    return (
        single(data_re, table_re) - single(data_im, table_im),
        single(data_im, table_re) + single(data_re, table_im),
    )


def forward_transform(signal, tables):
    (first_re, first_im), (twist_re, twist_im), (second_re, second_im) = tables
    section_re, section_im = apply_middle(first_re, first_im, signal)
    section_re, section_im = complex_product(section_re, section_im, twist_re, twist_im)
    return apply_last(second_re, second_im, section_re, section_im)


def inverse_transform(spec_re, spec_im, tables):
    (first_re, first_im), (twist_re, twist_im), (second_re, second_im) = tables
    section_re, section_im = apply_last(second_re, -second_im, spec_re, spec_im)
    section_re, section_im = complex_product(section_re, section_im, twist_re, -twist_im)
    result = jnp.einsum("kn,cnm->ckm", first_re, section_re, precision=HIGHEST) + jnp.einsum(
        "kn,cnm->ckm", first_im, section_im, precision=HIGHEST
    )
    total = first_re.shape[0] * second_re.shape[0]
    return result / float(total)


def padded_grid(signal, fft_rows, fft_cols):
    channels, seq_len = signal.shape
    padded = jnp.concatenate(
        [signal, jnp.zeros((channels, fft_rows * fft_cols - seq_len), jnp.float32)], axis=1
    )
    return padded.reshape(channels, fft_rows, fft_cols)


def leading_part(grid, seq_len):
    return grid.reshape(grid.shape[0], -1)[:, :seq_len]


def channels_first(block):
    return block[0].astype(jnp.float32).T


def rounded_sum(terms):
    rounded = lax.optimization_barrier(terms.astype(jnp.bfloat16))
    return jnp.sum(rounded.astype(jnp.float32), axis=0)


def axis_pairs(size, mask):
    return [(index, index ^ mask) for index in range(size)]


def ctx_masks(size):
    bits = [1 << b for b in range(size.bit_length() - 1)]
    low = [m for m in bits if m < 4]
    high = [m for m in bits if m >= 4]
    return tuple(reversed(high[1:])) + tuple(reversed(low[1:])) + tuple(high[:1]) + tuple(low[:1])


def doubling_gather(block, axis, masks):
    size = lax.axis_size(axis)
    held = block
    for mask in masks:
        held = jnp.concatenate([held, lax.ppermute(held, axis, axis_pairs(size, mask))], axis=0)
    return held


def unpermute_blocks(rows, axis, masks):
    size = lax.axis_size(axis)
    me = lax.axis_index(axis)
    wanted = me ^ jnp.arange(size, dtype=jnp.int32)
    place = jnp.zeros_like(wanted)
    for step, mask in enumerate(masks):
        place = place | (wanted & mask != 0).astype(jnp.int32) << step
    blocks = rows.reshape(size, rows.shape[0] // size, rows.shape[1])
    return jnp.take(blocks, place, axis=0).reshape(rows.shape)


def dp_masks(size):
    bits = [1 << b for b in range(size.bit_length() - 1)]
    return tuple(bits[:1]) + tuple(bits[2:]) + tuple(bits[1:2])


def summed_over_dp(grad_weight, grad_residues, grad_decays):
    size = lax.axis_size("dp")
    width = grad_weight.shape[1]
    extra = jnp.stack([grad_residues.reshape(-1), grad_decays.reshape(-1)])
    extra = jnp.pad(extra, ((0, 0), (0, width - extra.shape[1])))
    rows = grad_weight.shape[0] + 2
    padded_rows = -(-rows // size) * size
    held = jnp.concatenate(
        [grad_weight, extra, jnp.zeros((padded_rows - rows, width), jnp.float32)], axis=0
    )
    me = lax.axis_index("dp")
    masks = dp_masks(size)
    for mask in masks:
        half = held.shape[0] // 2
        low, high = (held[:half], held[half:])
        upper = me & mask != 0
        keep = jnp.where(upper, high, low)
        send = jnp.where(upper, low, high)
        held = keep + lax.ppermute(send, "dp", axis_pairs(size, mask))
    for mask in reversed(masks):
        other = lax.ppermute(held, "dp", axis_pairs(size, mask))
        upper = me & mask != 0
        held = jnp.where(upper, jnp.concatenate([other, held]), jnp.concatenate([held, other]))
    count = grad_residues.size
    weight = held[: grad_weight.shape[0]]
    residue_sum = held[grad_weight.shape[0], :count].reshape(grad_residues.shape)
    decay_sum = held[grad_weight.shape[0] + 1, :count].reshape(grad_decays.shape)
    return (weight, residue_sum, decay_sum)


def body(queries, keys, values, grad_out, out_weight, residues, decays):
    channels = out_weight.shape[0]
    block_width = out_weight.shape[1]
    tok_rows = grad_out.shape[1]
    grad_cols = lax.all_to_all(grad_out, "ctx", split_axis=2, concat_axis=1, tiled=True)
    shard_piece = lax.all_gather(out_weight, "ctx", axis=1, tiled=True)
    blocks = shard_piece.shape[1] // block_width
    partial_value = grad_out[0]
    partial_value = partial_value.reshape(tok_rows, blocks, block_width)
    weight_part = shard_piece.reshape(channels, blocks, block_width)
    terms = jnp.einsum(
        "tks,cks->ktc", partial_value, weight_part, preferred_element_type=jnp.float32
    )
    gated_sum = rounded_sum(terms)
    grad_gated = gated_sum.astype(jnp.bfloat16)[None]
    query_ch, key_ch, value_ch, gated_grad_ch = (
        lax.all_to_all(queries, "ctx", split_axis=2, concat_axis=1, tiled=True),
        lax.all_to_all(keys, "ctx", split_axis=2, concat_axis=1, tiled=True),
        lax.all_to_all(values, "ctx", split_axis=2, concat_axis=1, tiled=True),
        lax.all_to_all(grad_gated, "ctx", split_axis=2, concat_axis=1, tiled=True),
    )
    grad_gated_full = channels_first(gated_grad_ch)
    seq_len = query_ch.shape[1]
    fft_rows = 2 * seq_len // FFT_COLS
    tables = fourier_tables(fft_rows, FFT_COLS)
    query_full = channels_first(query_ch)
    key_full = channels_first(key_ch)
    value_full = channels_first(value_ch)
    positions = jnp.arange(seq_len).astype(jnp.float32)
    decay_terms = jnp.exp(-decays[:, :, None] * positions[None, None, :])
    filter_taps = jnp.sum(residues[:, :, None] * decay_terms, axis=1)
    product = key_full * value_full
    grad_conv = grad_gated_full * query_full
    prod_re, prod_im = forward_transform(padded_grid(product, fft_rows, FFT_COLS), tables)
    taps_re, taps_im = forward_transform(padded_grid(filter_taps, fft_rows, FFT_COLS), tables)
    grad_re, grad_im = forward_transform(padded_grid(grad_conv, fft_rows, FFT_COLS), tables)
    conv_out = leading_part(
        inverse_transform(*complex_product(prod_re, prod_im, taps_re, taps_im), tables), seq_len
    )
    grad_product = leading_part(
        inverse_transform(*complex_product(taps_re, -taps_im, grad_re, grad_im), tables), seq_len
    )
    grad_taps = leading_part(
        inverse_transform(*complex_product(prod_re, -prod_im, grad_re, grad_im), tables), seq_len
    )
    gated_t = (query_full * conv_out).astype(jnp.bfloat16)
    grad_queries = (grad_gated_full * conv_out).T.astype(jnp.bfloat16)[None]
    grad_keys = (grad_product * value_full).T.astype(jnp.bfloat16)[None]
    grad_values = (grad_product * key_full).T.astype(jnp.bfloat16)[None]
    ctx_size = lax.axis_size("ctx")
    gather_masks = ctx_masks(ctx_size)
    gathered = doubling_gather(gated_t, "ctx", gather_masks)
    partial_value = lax.dot_general(
        gathered, grad_cols[0], (((1,), (0,)), ((), ())), preferred_element_type=jnp.float32
    )
    grad_weight = unpermute_blocks(partial_value, "ctx", gather_masks)
    grad_residues = jnp.sum(grad_taps[:, None, :] * decay_terms, axis=2)
    grad_decays = -residues * jnp.sum(
        (grad_taps * positions[None, :])[:, None, :] * decay_terms, axis=2
    )
    grad_weight, grad_residues, grad_decays = summed_over_dp(
        grad_weight, grad_residues, grad_decays
    )
    return (grad_queries, grad_keys, grad_values, grad_weight, grad_residues, grad_decays)


def solution(mesh):
    placed = (
        P("dp", "ctx", None),
        P("dp", "ctx", None),
        P("dp", "ctx", None),
        P("dp", "ctx", None),
        P(None, "ctx"),
        P("ctx", None),
        P("ctx", None),
    )
    return jax.shard_map(
        body,
        mesh=mesh,
        in_specs=placed,
        out_specs=(
            P("dp", None, "ctx"),
            P("dp", None, "ctx"),
            P("dp", None, "ctx"),
            P(None, "ctx"),
            P("ctx", None),
            P("ctx", None),
        ),
        check_vma=False,
    )
```

profile of v0, /device:TPU:107, one launch (start us, length us, event | category | flops | bytes accessed | tf_op | source)
XLA Modules:
  0.0 560.3 jit_solution(7011197182111758625)
XLA Ops:
  7.2 1.8 copy.70
  9.0 1.1 copy.82
  10.6 1.4 reduce.11
  12.7 10.7 %all-to-all-start.3 = ((bf16[32,2,1024]{2,1,0:T(2,128)(2,1)}), bf16[32,2,1024]{2,1,0:T(2,128)(2,1)S(1)}, u32[]{:S(2)}, u32[]{:S(2)}) async-start(bf16[32,2,1024]{2,1,0:T(2,128)(2,1)} %reshape.256), calls=%async_computation.3 | async-start | bytes 262144 | tf_op jit(solution)/shard_map/all_to_all | solution.py:174
  23.4 1.1 copy.76
  24.5 1.4 reduce.10
  26.6 4.8 all-to-all-done.3
  31.4 5.9 %all-to-all-start.1 = ((bf16[32,2,1024]{2,1,0:T(2,128)(2,1)}), bf16[32,2,1024]{2,1,0:T(2,128)(2,1)S(1)}, u32[]{:S(2)}, u32[]{:S(2)}) async-start(bf16[32,2,1024]{2,1,0:T(2,128)(2,1)} %reshape.254), calls=%async_computation.1 | async-start | bytes 262144 | tf_op jit(solution)/shard_map/all_to_all | solution.py:175
  38.0 1.1 copy.79
  39.1 1.4 reduce.9
  41.2 2.2 copy.89
  43.8 3.4 all-to-all-done.1
  47.2 7.3 %all-to-all-start.2 = ((bf16[32,2,1024]{2,1,0:T(2,128)(2,1)}), bf16[32,2,1024]{2,1,0:T(2,128)(2,1)S(1)}, u32[]{:S(2)}, u32[]{:S(2)}) async-start(bf16[32,2,1024]{2,1,0:T(2,128)(2,1)} %reshape.252), calls=%async_computation.2 | async-start | bytes 262144 | tf_op jit(solution)/shard_map/all_to_all | solution.py:176
  54.9 9.4 %all-to-all-done.2 = bf16[32,2,1024]{2,1,0:T(2,128)(2,1)S(1)} async-done(((bf16[32,2,1024]{2,1,0:T(2,128)(2,1)}), bf16[32,2,1024]{2,1,0:T(2,128)(2,1)S(1)}, u32[]{:S(2)}, u32[]{:S(2)}) %all-to-all-start.2) | async-done | bytes 131104 | tf_op jit(solution)/shard_map/all_to_all | solution.py:176
  67.5 1.6 fusion.48
  69.2 1.7 convolution_add_fusion.8
  70.8 139.5 %all-gather.2.cloned.1.call-done = bf16[512,8192]{0,1:T(8,128)(2,1)} async-done(((bf16[512,256]{0,1:T(8,128)(2,1)}), bf16[512,8192]{0,1:T(8,128)(2,1)}) %all-gather.2.cloned.1.call-update) | async-done | bytes 8388624 | tf_op jit(solution)/shard_map/all_gather | solution.py:163
  210.3 8.2 %convolution_convert_fusion = bf16[32,128,512]{2,1,0:T(8,128)(2,1)} fusion(bf16[512,32,256]{0,2,1:T(8,128)(2,1)} %bitcast.286, bf16[128,32,256]{2,1,0:T(8,128)(2,1)S(1)} %bitcast.287), kind=kOutput, calls=%fused_computation.5 | convolution fusion | flops 1075838976 | bytes 14680064 | tf_op jit(solution)/shard_map/tks,cks->ktc/dot_general | solution.py:168
  218.5 2.9 reduce_sum.39
  221.5 1.4 reduce.12
  223.6 9.0 %all-to-all-start = ((bf16[32,2,1024]{2,1,0:T(2,128)(2,1)}), bf16[32,2,1024]{2,1,0:T(2,128)(2,1)S(1)}, u32[]{:S(2)}, u32[]{:S(2)}) async-start(bf16[32,2,1024]{2,1,0:T(2,128)(2,1)} %reshape.258), calls=%async_computation | async-start | bytes 262144 | tf_op jit(solution)/shard_map/all_to_all | solution.py:177
  233.5 6.9 %all-to-all-done = bf16[32,2,1024]{2,1,0:T(2,128)(2,1)S(1)} async-done(((bf16[32,2,1024]{2,1,0:T(2,128)(2,1)}), bf16[32,2,1024]{2,1,0:T(2,128)(2,1)S(1)}, u32[]{:S(2)}, u32[]{:S(2)}) %all-to-all-start) | async-done | bytes 131104 | tf_op jit(solution)/shard_map/all_to_all | solution.py:177
  245.1 0.9 multiply_subtract_fusion
  251.3 2.5 multiply_reduce_fusion.1
  257.9 1.1 multiply_subtract_fusion.1
  265.0 3.1 collective-permute-start
  268.2 7.2 %collective-permute-done = bf16[16,4096]{1,0:T(8,128)(2,1)S(1)} collective-permute-done((bf16[16,4096]{1,0:T(8,128)(2,1)S(1)}, bf16[16,4096]{1,0:T(8,128)(2,1)S(1)}, u32[]{:S(2)}, u32[]{:S(2)}) %collective-permute-start) | collective-permute-done | bytes 131104 | tf_op jit(solution)/shard_map/ppermute | solution.py:108
  275.5 3.6 collective-permute-start.1
  279.0 10.0 %collective-permute-done.1 = bf16[32,4096]{1,0:T(8,128)(2,1)S(1)} collective-permute-done((bf16[32,4096]{1,0:T(8,128)(2,1)S(1)}, bf16[32,4096]{1,0:T(8,128)(2,1)S(1)}, u32[]{:S(2)}, u32[]{:S(2)}) %collective-permute-start.1) | collective-permute-done | bytes 262176 | tf_op jit(solution)/shard_map/ppermute | solution.py:108
  290.5 2.0 collective-permute-start.2
  292.6 7.1 %copy.85 = bf16[1,128,8192]{1,0,2:T(2,128)(2,1)} copy(bf16[1,128,8192]{2,1,0:T(8,128)(2,1)S(1)} %copy-done) | data formatting | bytes 4194304 | tf_op args[3]
  299.6 45.2 %reduce.13 = bf16[8192,128]{1,0:T(8,128)(2,1)S(1)} reduce(bf16[8192,1,128]{2,1,0:T(2,128)(2,1)} %bitcast.288, bf16[]{:T(256)} %broadcast.471), dimensions={1}, to_apply=%bitcast.254.reduce_sub_computation | reduce | bytes 4194306
  344.8 2.1 reshape.260
  346.9 8.6 %all-to-all-start.4 = ((bf16[32,2,16384]{2,1,0:T(2,128)(2,1)}), bf16[32,2,16384]{2,1,0:T(2,128)(2,1)S(1)}, u32[]{:S(2)}, u32[]{:S(2)}) async-start(bf16[32,2,16384]{2,1,0:T(2,128)(2,1)} %reshape.260), calls=%async_computation.4 | async-start | bytes 4194304 | tf_op jit(solution)/shard_map/all_to_all | solution.py:162
  355.5 1.2 pad_maximum_fusion
  356.7 2.2 collective-permute-start.3
  359.5 1.7 constant_dynamic-update-slice_fusion.2
  361.2 1.9 constant_dynamic-update-slice_fusion.1
  363.2 67.6 %collective-permute-done.3 = bf16[128,4096]{1,0:T(8,128)(2,1)S(1)} collective-permute-done((bf16[128,4096]{1,0:T(8,128)(2,1)S(1)}, bf16[128,4096]{1,0:T(8,128)(2,1)S(1)}, u32[]{:S(2)}, u32[]{:S(2)}) %collective-permute-start.3) | collective-permute-done | bytes 1048608 | tf_op jit(solution)/shard_map/ppermute | solution.py:108
  430.8 1.2 constant_dynamic-update-slice_fusion
  431.9 1.9 copy-done.16
  433.9 1.9 collective-permute-start.4
  436.1 6.8 %reshape.261 = bf16[8192,1,128]{2,1,0:T(2,128)(2,1)} reshape(bf16[32,2,16384]{2,1,0:T(2,128)(2,1)S(1)} %all-to-all-done.4) | data formatting | bytes 4194304
  442.9 2.5 copy.88
  445.4 2.9 copy.86
  448.5 32.8 %collective-permute-done.4 = bf16[256,4096]{1,0:T(8,128)(2,1)} collective-permute-done((bf16[256,4096]{1,0:T(8,128)(2,1)}, bf16[256,4096]{1,0:T(8,128)(2,1)}, u32[]{:S(2)}, u32[]{:S(2)}) %collective-permute-start.4) | collective-permute-done | bytes 2097184 | tf_op jit(solution)/shard_map/ppermute | solution.py:108
  481.3 3.1 constant_dynamic-update-slice_fusion.5
  484.4 4.2 fusion.323
  488.7 1.6 gather_fusion
  490.6 4.7 collective-permute-start.5
  496.6 1.9 collective-permute-start.6
  499.3 4.0 collective-permute-done.6
  503.4 2.4 collective-permute-start.7
  506.6 3.5 collective-permute-done.7
  510.2 2.3 collective-permute-start.8
  513.3 5.7 %collective-permute-done.8 = f32[33,256]{1,0:T(8,128)S(1)} collective-permute-done((f32[33,256]{1,0:T(8,128)S(1)}, f32[33,256]{1,0:T(8,128)S(1)}, u32[]{:S(2)}, u32[]{:S(2)}) %collective-permute-start.8) | collective-permute-done | bytes 33824 | tf_op jit(solution)/shard_map/ppermute | solution.py:146
  519.0 1.9 collective-permute-start.9
  521.7 5.9 %collective-permute-done.9 = f32[33,256]{1,0:T(8,128)S(1)} collective-permute-done((f32[33,256]{1,0:T(8,128)S(1)}, f32[33,256]{1,0:T(8,128)S(1)}, u32[]{:S(2)}, u32[]{:S(2)}) %collective-permute-start.9) | collective-permute-done | bytes 33824 | tf_op jit(solution)/shard_map/ppermute | solution.py:148
  527.7 2.3 collective-permute-start.10
  531.0 3.2 collective-permute-done.10
  534.3 2.6 collective-permute-start.11
  536.9 1.0 fusion.55
  538.0 2.4 collective-permute-done.11
  540.4 9.4 %collective-permute-start.12 = (f32[264,256]{1,0:T(8,128)S(1)}, f32[264,256]{1,0:T(8,128)S(1)}, u32[]{:S(2)}, u32[]{:S(2)}) collective-permute-start(f32[264,256]{1,0:T(8,128)S(1)} %maximum_select_fusion.1), channel_id=1, source_target_pairs={{0,32},{32,0},{64,96},{96,64},{128,160},{160,128},{192,224},{224,1... | collective-permute-start | bytes 811016 | tf_op jit(solution)/shard_map/ppermute | solution.py:148
  (142 shorter events, 40.8 us)
Async XLA Ops:
  7.2 203.1 %all-gather.2.cloned.1.call-start = ((), (), s32[]{:S(2)}) async-start(), calls=%async_computation.5 | async-start | bytes 8650752 | tf_op jit(solution)/shard_map/all_gather | solution.py:163
  12.7 18.6 %all-to-all-start.3 = ((bf16[32,2,1024]{2,1,0:T(2,128)(2,1)}), bf16[32,2,1024]{2,1,0:T(2,128)(2,1)S(1)}, u32[]{:S(2)}, u32[]{:S(2)}) async-start(bf16[32,2,1024]{2,1,0:T(2,128)(2,1)} %reshape.256), calls=%async_computation.3 | async-start | bytes 262144 | tf_op jit(solution)/shard_map/all_to_all | solution.py:174
  31.4 15.8 %all-to-all-start.1 = ((bf16[32,2,1024]{2,1,0:T(2,128)(2,1)}), bf16[32,2,1024]{2,1,0:T(2,128)(2,1)S(1)}, u32[]{:S(2)}, u32[]{:S(2)}) async-start(bf16[32,2,1024]{2,1,0:T(2,128)(2,1)} %reshape.254), calls=%async_computation.1 | async-start | bytes 262144 | tf_op jit(solution)/shard_map/all_to_all | solution.py:175
  47.2 17.1 %all-to-all-start.2 = ((bf16[32,2,1024]{2,1,0:T(2,128)(2,1)}), bf16[32,2,1024]{2,1,0:T(2,128)(2,1)S(1)}, u32[]{:S(2)}, u32[]{:S(2)}) async-start(bf16[32,2,1024]{2,1,0:T(2,128)(2,1)} %reshape.252), calls=%async_computation.2 | async-start | bytes 262144 | tf_op jit(solution)/shard_map/all_to_all | solution.py:176
  54.6 186.1 %copy-start.2 = (f32[1,32,128,16]{2,1,3,0:T(8,128)}, f32[1,32,128,16]{2,1,3,0:T(8,128)S(1)}, u32[]{:S(2)}) copy-start(f32[1,32,128,16]{2,1,3,0:T(8,128)S(1)} %copy.84) | copy-start | bytes 786436
  54.9 10.2 %copy-start.6 = (f32[1,32,128,16]{2,1,3,0:T(8,128)}, f32[1,32,128,16]{2,1,3,0:T(8,128)S(1)}, u32[]{:S(2)}) copy-start(f32[1,32,128,16]{2,1,3,0:T(8,128)S(1)} %copy.78) | copy-start | bytes 786436
  64.6 0.7 copy-start.8
  218.5 14.1 %copy-start.14 = (f32[16,64,128]{2,1,0:T(8,128)S(1)}, f32[16,64,128]{2,1,0:T(8,128)}, u32[]{:S(2)}) copy-start(f32[16,64,128]{2,1,0:T(8,128)} %fusion.48) | copy-start | bytes 1572868
  223.6 16.8 %all-to-all-start = ((bf16[32,2,1024]{2,1,0:T(2,128)(2,1)}), bf16[32,2,1024]{2,1,0:T(2,128)(2,1)S(1)}, u32[]{:S(2)}, u32[]{:S(2)}) async-start(bf16[32,2,1024]{2,1,0:T(2,128)(2,1)} %reshape.258), calls=%async_computation | async-start | bytes 262144 | tf_op jit(solution)/shard_map/all_to_all | solution.py:177
  240.7 4.5 copy-start.4
  241.0 4.1 copy-start.1
  247.7 3.6 copy-start.15
  260.6 3.6 copy-start.3
  261.4 31.1 %copy-start = (bf16[1,128,8192]{2,1,0:T(8,128)(2,1)S(1)}, bf16[1,128,8192]{2,1,0:T(8,128)(2,1)}, u32[]{:S(2)}) copy-start(bf16[1,128,8192]{2,1,0:T(8,128)(2,1)} %param.10) | copy-start | bytes 6291460
  264.2 11.3 %copy-start.11 = (f32[2,8,64,128]{3,1,2,0:T(8,128)}, f32[2,8,64,128]{3,1,2,0:T(8,128)S(1)}, u32[]{:S(2)}) copy-start(f32[2,8,64,128]{3,1,2,0:T(8,128)S(1)} %copy.122) | copy-start | bytes 1572868
  265.0 10.4 %collective-permute-start = (bf16[16,4096]{1,0:T(8,128)(2,1)S(1)}, bf16[16,4096]{1,0:T(8,128)(2,1)S(1)}, u32[]{:S(2)}, u32[]{:S(2)}) collective-permute-start(bf16[16,4096]{1,0:T(8,128)(2,1)S(1)} %get-tuple-element.12), channel_id=1, source_target_pairs={{0,16},{1,17},{2,18},{3,19},{4,20},{5,21},{6,22},{7,23},{8,24},{9,... | collective-permute-start | bytes 393224 | tf_op jit(solution)/shard_map/ppermute | solution.py:108
  275.5 13.5 %collective-permute-start.1 = (bf16[32,4096]{1,0:T(8,128)(2,1)S(1)}, bf16[32,4096]{1,0:T(8,128)(2,1)S(1)}, u32[]{:S(2)}, u32[]{:S(2)}) collective-permute-start(bf16[32,4096]{1,0:T(8,128)(2,1)S(1)} %pad_maximum_fusion.4), channel_id=1, source_target_pairs={{0,8},{1,9},{2,10},{3,11},{4,12},{5,13},{6,14},{7,15},{8,0},{9,1},... | collective-permute-start | bytes 786440 | tf_op jit(solution)/shard_map/ppermute | solution.py:108
  289.0 0.7 copy-start.10
  290.5 64.9 %collective-permute-start.2 = (bf16[64,4096]{1,0:T(8,128)(2,1)}, bf16[64,4096]{1,0:T(8,128)(2,1)}, u32[]{:S(2)}, u32[]{:S(2)}) collective-permute-start(bf16[64,4096]{1,0:T(8,128)(2,1)} %pad_maximum_fusion.1), channel_id=1, source_target_pairs={{0,2},{1,3},{2,0},{3,1},{4,6},{5,7},{6,4},{7,5},{8,10},{9,11},{10,... | collective-permute-start | bytes 1572872 | tf_op jit(solution)/shard_map/ppermute | solution.py:108
  346.9 89.2 %all-to-all-start.4 = ((bf16[32,2,16384]{2,1,0:T(2,128)(2,1)}), bf16[32,2,16384]{2,1,0:T(2,128)(2,1)S(1)}, u32[]{:S(2)}, u32[]{:S(2)}) async-start(bf16[32,2,16384]{2,1,0:T(2,128)(2,1)} %reshape.260), calls=%async_computation.4 | async-start | bytes 4194304 | tf_op jit(solution)/shard_map/all_to_all | solution.py:162
  356.7 74.1 %collective-permute-start.3 = (bf16[128,4096]{1,0:T(8,128)(2,1)S(1)}, bf16[128,4096]{1,0:T(8,128)(2,1)S(1)}, u32[]{:S(2)}, u32[]{:S(2)}) collective-permute-start(bf16[128,4096]{1,0:T(8,128)(2,1)S(1)} %pad_maximum_fusion), channel_id=1, source_target_pairs={{0,4},{1,5},{2,6},{3,7},{4,0},{5,1},{6,2},{7,3},{8,12},{9,13},{10,... | collective-permute-start | bytes 3145736 | tf_op jit(solution)/shard_map/ppermute | solution.py:108
  431.9 1.9 copy-start.16
  433.9 47.5 %collective-permute-start.4 = (bf16[256,4096]{1,0:T(8,128)(2,1)}, bf16[256,4096]{1,0:T(8,128)(2,1)}, u32[]{:S(2)}, u32[]{:S(2)}) collective-permute-start(bf16[256,4096]{1,0:T(8,128)(2,1)} %get-tuple-element.19), channel_id=1, source_target_pairs={{0,1},{1,0},{2,3},{3,2},{4,5},{5,4},{6,7},{7,6},{8,9},{9,8},{10,11... | collective-permute-start | bytes 6291464 | tf_op jit(solution)/shard_map/ppermute | solution.py:108
  448.3 36.1 %copy-start.13 = (bf16[1,32,128,256]{3,2,1,0:T(8,128)(2,1)S(1)}, bf16[1,32,128,256]{3,2,1,0:T(8,128)(2,1)}, u32[]{:S(2)}) copy-start(bf16[1,32,128,256]{3,2,1,0:T(8,128)(2,1)} %copy.86) | copy-start | bytes 6291460
  490.6 5.9 %collective-permute-start.5 = (f32[264,256]{1,0:T(8,128)S(1)}, f32[264,256]{1,0:T(8,128)S(1)}, u32[]{:S(2)}, u32[]{:S(2)}) collective-permute-start(f32[264,256]{1,0:T(8,128)S(1)} %slice_select_fusion), channel_id=1, source_target_pairs={{0,32},{32,0},{64,96},{96,64},{128,160},{160,128},{192,224},{224,1... | collective-permute-start | bytes 811016 | tf_op jit(solution)/shard_map/ppermute | solution.py:146
  496.6 6.8 %collective-permute-start.6 = (f32[132,256]{1,0:T(8,128)S(1)}, f32[132,256]{1,0:T(8,128)S(1)}, u32[]{:S(2)}, u32[]{:S(2)}) collective-permute-start(f32[132,256]{1,0:T(8,128)S(1)} %slice_select_fusion.1), channel_id=1, source_target_pairs={{0,128},{32,160},{64,192},{96,224},{128,0},{160,32},{192,64},{224,... | collective-permute-start | bytes 405512 | tf_op jit(solution)/shard_map/ppermute | solution.py:146
  503.4 33.6 %copy-start.7 = (f32[1,32,128,16]{2,1,3,0:T(8,128)S(1)}, f32[1,32,128,16]{2,1,3,0:T(8,128)}, u32[]{:S(2)}) copy-start(f32[1,32,128,16]{2,1,3,0:T(8,128)} %copy-done.6) | copy-start | bytes 786436
  503.4 33.6 %copy-start.9 = (f32[1,32,128,16]{2,1,3,0:T(8,128)S(1)}, f32[1,32,128,16]{2,1,3,0:T(8,128)}, u32[]{:S(2)}) copy-start(f32[1,32,128,16]{2,1,3,0:T(8,128)} %copy-done.8) | copy-start | bytes 786436
  503.4 6.7 %collective-permute-start.7 = (f32[66,256]{1,0:T(8,128)S(1)}, f32[66,256]{1,0:T(8,128)S(1)}, u32[]{:S(2)}, u32[]{:S(2)}) collective-permute-start(f32[66,256]{1,0:T(8,128)S(1)} %slice_select_fusion.2), channel_id=1, source_target_pairs={{0,256},{32,288},{64,320},{96,352},{128,384},{160,416},{192,448},{... | collective-permute-start | bytes 202760 | tf_op jit(solution)/shard_map/ppermute | solution.py:146
  510.2 39.6 %copy-start.5 = (f32[1,32,128,16]{2,1,3,0:T(8,128)S(1)}, f32[1,32,128,16]{2,1,3,0:T(8,128)}, u32[]{:S(2)}) copy-start(f32[1,32,128,16]{2,1,3,0:T(8,128)} %copy-done.4) | copy-start | bytes 786436
  510.2 39.6 %copy-start.12 = (f32[2,8,64,128]{3,1,2,0:T(8,128)S(1)}, f32[2,8,64,128]{3,1,2,0:T(8,128)}, u32[]{:S(2)}) copy-start(f32[2,8,64,128]{3,1,2,0:T(8,128)} %copy-done.11) | copy-start | bytes 1572868
  510.2 8.8 %collective-permute-start.8 = (f32[33,256]{1,0:T(8,128)S(1)}, f32[33,256]{1,0:T(8,128)S(1)}, u32[]{:S(2)}, u32[]{:S(2)}) collective-permute-start(f32[33,256]{1,0:T(8,128)S(1)} %slice_select_fusion.3), channel_id=1, source_target_pairs={{0,64},{32,96},{64,0},{96,32},{128,192},{160,224},{192,128},{224,1... | collective-permute-start | bytes 101384 | tf_op jit(solution)/shard_map/ppermute | solution.py:146
  519.0 8.7 %collective-permute-start.9 = (f32[33,256]{1,0:T(8,128)S(1)}, f32[33,256]{1,0:T(8,128)S(1)}, u32[]{:S(2)}, u32[]{:S(2)}) collective-permute-start(f32[33,256]{1,0:T(8,128)S(1)} %select_add_fusion.3), channel_id=1, source_target_pairs={{0,64},{32,96},{64,0},{96,32},{128,192},{160,224},{192,128},{224,1... | collective-permute-start | bytes 101384 | tf_op jit(solution)/shard_map/ppermute | solution.py:148
  527.7 6.6 %collective-permute-start.10 = (f32[66,256]{1,0:T(8,128)S(1)}, f32[66,256]{1,0:T(8,128)S(1)}, u32[]{:S(2)}, u32[]{:S(2)}) collective-permute-start(f32[66,256]{1,0:T(8,128)S(1)} %maximum_select_fusion.3), channel_id=1, source_target_pairs={{0,256},{32,288},{64,320},{96,352},{128,384},{160,416},{192,448},{... | collective-permute-start | bytes 202760 | tf_op jit(solution)/shard_map/ppermute | solution.py:148
  534.3 6.1 %collective-permute-start.11 = (f32[132,256]{1,0:T(8,128)S(1)}, f32[132,256]{1,0:T(8,128)S(1)}, u32[]{:S(2)}, u32[]{:S(2)}) collective-permute-start(f32[132,256]{1,0:T(8,128)S(1)} %maximum_select_fusion.2), channel_id=1, source_target_pairs={{0,128},{32,160},{64,192},{96,224},{128,0},{160,32},{192,64},{224,... | collective-permute-start | bytes 405512 | tf_op jit(solution)/shard_map/ppermute | solution.py:148
  540.4 10.5 %collective-permute-start.12 = (f32[264,256]{1,0:T(8,128)S(1)}, f32[264,256]{1,0:T(8,128)S(1)}, u32[]{:S(2)}, u32[]{:S(2)}) collective-permute-start(f32[264,256]{1,0:T(8,128)S(1)} %maximum_select_fusion.1), channel_id=1, source_target_pairs={{0,32},{32,0},{64,96},{96,64},{128,160},{160,128},{192,224},{224,1... | collective-permute-start | bytes 811016 | tf_op jit(solution)/shard_map/ppermute | solution.py:148
Sparse Core Ops, SparseCore 0:
  10.1 200.2 all-gather.1
where the time goes:
time: 566 us; the launch traced here: 560 us
  waiting for transfers between devices  307 us (54%)
  starting transfers between devices  81.8 us (14%)
  other arithmetic  63.1 us (11%)
  local copies, waits for them, and re-layouts  49.9 us (9%)
  matrix products  43.1 us (8%)
  between operations  15.3 us (3%)
    all_gather x1, waiting for transfers between devices, body(): shard_piece = lax.all_gather(out_weight, 'ctx', axis=1, tiled=True)  139 us
    ppermute x5, waiting for transfers between devices, doubling_gather(): lax.ppermute(held, axis, axis_pairs(size, mask))  118 us
    unnamed x6, other arithmetic  51.7 us
    unnamed x65, local copies, waits for them, and re-layouts  37.9 us
    dot_general x24, matrix products, single(): return jnp.einsum('ckm,mj->ckj', data, table, precision=HIGHEST)  21.6 us
    ppermute x4, starting transfers between devices, summed_over_dp(): other = lax.ppermute(held, 'dp', axis_pairs(size, mask))  16.2 us
    ppermute x4, waiting for transfers between devices, summed_over_dp(): held = keep + lax.ppermute(send, 'dp', axis_pairs(size, mask))  13.5 us
    ppermute x5, starting transfers between devices, doubling_gather(): lax.ppermute(held, axis, axis_pairs(size, mask))  12.8 us
  transfers between devices with their start and end apart: 19, of which 17 were waited for; matrix products, arithmetic and copies ran while one was open for 18% of the time, Pallas kernels for 0%

commit v1 on v0

--- a/solution.py
+++ b/solution.py
@@ -6,6 +6,9 @@
 
 FFT_COLS = 128
 HIGHEST = lax.Precision.HIGHEST
+spot_push = lambda x_part, shard_axis: jnp.concatenate(
+    lax.all_to_all(jnp.stack(lax.axis_size(shard_axis) * [x_part]), shard_axis, 0, 0), 1
+)
 
 
 def fourier_tables(fft_rows, fft_cols):
@@ -160,7 +163,7 @@
     block_width = out_weight.shape[1]
     tok_rows = grad_out.shape[1]
     grad_cols = lax.all_to_all(grad_out, "ctx", split_axis=2, concat_axis=1, tiled=True)
-    shard_piece = lax.all_gather(out_weight, "ctx", axis=1, tiled=True)
+    shard_piece = spot_push(out_weight, "ctx")
     blocks = shard_piece.shape[1] // block_width
     partial_value = grad_out[0]
     partial_value = partial_value.reshape(tok_rows, blocks, block_width)

time: 566 us -> 674 us (1.19)
  the two profiles are of different devices: /device:TPU:107 before, /device:TPU:63 now
where the time goes in v1:
time: 674 us; the launch traced here: 669 us
  waiting for transfers between devices  353 us (52%)
  starting transfers between devices  136 us (20%)
  other arithmetic  64.6 us (10%)
  local copies, waits for them, and re-layouts  54.1 us (8%)
  matrix products  46.1 us (7%)
  blocking collectives  12.6 us (2%)
    all_to_all x1, waiting for transfers between devices, lax.all_to_all(jnp.stack(lax.axis_size(shard_axis) * [x_part]), shard_axi...  197 us
    ppermute x5, waiting for transfers between devices, doubling_gather(): lax.ppermute(held, axis, axis_pairs(size, mask))  117 us
    all_to_all x1, starting transfers between devices, body(): lax.all_to_all(grad_gated, 'ctx', split_axis=2, concat_axis=1, tiled=True)  63.2 us
    unnamed x6, other arithmetic  53.2 us
    unnamed x62, local copies, waits for them, and re-layouts  36.3 us
    dot_general x24, matrix products, single(): return jnp.einsum('ckm,mj->ckj', data, table, precision=HIGHEST)  24.2 us
    ppermute x4, starting transfers between devices, summed_over_dp(): other = lax.ppermute(held, 'dp', axis_pairs(size, mask))  16 us
  transfers between devices with their start and end apart: 18, of which 16 were waited for; matrix products, arithmetic and copies ran while one was open for 14% of the time, Pallas kernels for 0%

profile of v1, /device:TPU:63, one launch (start us, length us, event | category | flops | bytes accessed | tf_op | source)
XLA Modules:
  0.0 668.8 jit_solution(4322629779818814089)
XLA Ops:
  0.6 1.1 copy.72
  2.2 1.4 reduce.11
  4.3 13.2 %all-to-all-start.4 = ((bf16[32,2,1024]{2,1,0:T(2,128)(2,1)}), bf16[32,2,1024]{2,1,0:T(2,128)(2,1)S(1)}, u32[]{:S(2)}, u32[]{:S(2)}) async-start(bf16[32,2,1024]{2,1,0:T(2,128)(2,1)} %reshape.258), calls=%async_computation.4 | async-start | bytes 262144 | tf_op jit(solution)/shard_map/all_to_all | solution.py:177
  17.5 1.1 copy.66
  18.6 1.4 reduce.10
  20.7 4.7 all-to-all-done.4
  25.4 5.8 all-to-all-start.2
  31.2 1.1 copy.69
  32.3 1.4 reduce.9
  33.7 5.4 all-to-all-done.2
  39.1 12.6 %all_to_all.56 = bf16[32,2,1024]{2,1,0:T(2,128)(2,1)S(1)} all-to-all(bf16[32,2,1024]{2,1,0:T(2,128)(2,1)S(1)} %reshape.254), channel_id=1, replica_groups=mesh['dp'=16,'ctx'=32] {'ctx'}, dimensions={0} | all-to-all | bytes 262144 | tf_op jit(solution)/shard_map/all_to_all | solution.py:179
  51.8 5.1 stack.2
  56.9 7.6 %all-to-all-start = ((bf16[32,512,256]{2,1,0:T(8,128)(2,1)}), bf16[32,512,256]{2,1,0:T(8,128)(2,1)}, u32[]{:S(2)}, u32[]{:S(2)}) async-start(bf16[32,512,256]{2,1,0:T(8,128)(2,1)} %stack.2), calls=%async_computation | async-start | bytes 16777216 | tf_op jit(solution)/shard_map/all_to_all | solution.py:10
  64.5 1.9 copy.78
  70.6 1.6 fusion.53
  72.2 1.6 convolution_add_fusion.8
  73.9 197.1 %all-to-all-done = bf16[32,512,256]{2,1,0:T(8,128)(2,1)} async-done(((bf16[32,512,256]{2,1,0:T(8,128)(2,1)}), bf16[32,512,256]{2,1,0:T(8,128)(2,1)}, u32[]{:S(2)}, u32[]{:S(2)}) %all-to-all-start) | async-done | bytes 8388640 | tf_op jit(solution)/shard_map/all_to_all | solution.py:10
  270.9 9.3 %fusion.2 = bf16[32,128,512]{2,1,0:T(8,128)(2,1)} fusion(bf16[32,512,256]{2,1,0:T(8,128)(2,1)} %all-to-all-done, bf16[128,32,256]{2,1,0:T(8,128)(2,1)} %bitcast.292), kind=kOutput, calls=%fused_computation.7 | convolution fusion | flops 1075838976 | bytes 14680064 | tf_op jit(solution)/shard_map/tks,cks->ktc/dot_general | solution.py:171
  280.2 3.5 reduce_sum.39
  283.7 1.8 copy.63
  285.5 3.0 reduce.12
  288.4 1.6 reshape.260
  290.0 63.2 %all-to-all-start.1 = ((bf16[32,2,1024]{2,1,0:T(2,128)(2,1)}), bf16[32,2,1024]{2,1,0:T(2,128)(2,1)}, u32[]{:S(2)}, u32[]{:S(2)}) async-start(bf16[32,2,1024]{2,1,0:T(2,128)(2,1)} %reshape.260), calls=%async_computation.1 | async-start | bytes 262144 | tf_op jit(solution)/shard_map/all_to_all | solution.py:180
  353.2 2.7 convolution_subtract_fusion.5
  355.9 5.2 all-to-all-done.1
  361.1 1.6 reshape.261
  373.9 2.6 multiply_reduce_fusion.1
  380.6 1.9 multiply_subtract_fusion.1
  388.5 2.1 collective-permute-start
  390.7 7.5 %collective-permute-done = bf16[16,4096]{1,0:T(8,128)(2,1)S(1)} collective-permute-done((bf16[16,4096]{1,0:T(8,128)(2,1)S(1)}, bf16[16,4096]{1,0:T(8,128)(2,1)S(1)}, u32[]{:S(2)}, u32[]{:S(2)}) %collective-permute-start) | collective-permute-done | bytes 131104 | tf_op jit(solution)/shard_map/ppermute | solution.py:111
  398.3 1.9 collective-permute-start.1
  400.2 12.3 %collective-permute-done.1 = bf16[32,4096]{1,0:T(8,128)(2,1)S(1)} collective-permute-done((bf16[32,4096]{1,0:T(8,128)(2,1)S(1)}, bf16[32,4096]{1,0:T(8,128)(2,1)S(1)}, u32[]{:S(2)}, u32[]{:S(2)}) %collective-permute-start.1) | collective-permute-done | bytes 262176 | tf_op jit(solution)/shard_map/ppermute | solution.py:111
  413.4 3.3 collective-permute-start.2
  416.7 7.0 %copy.75 = bf16[1,128,8192]{1,0,2:T(2,128)(2,1)} copy(bf16[1,128,8192]{2,1,0:T(8,128)(2,1)S(1)} %copy-done) | data formatting | bytes 4194304 | tf_op args[3]
  423.7 45.2 %reduce.13 = bf16[8192,128]{1,0:T(8,128)(2,1)S(1)} reduce(bf16[8192,1,128]{2,1,0:T(2,128)(2,1)} %bitcast.289, bf16[]{:T(256)} %broadcast.473), dimensions={1}, to_apply=%bitcast.258.reduce_sub_computation | reduce | bytes 4194306
  468.9 2.1 reshape.262
  471.0 6.1 all-to-all-start.5
  477.1 1.1 pad_maximum_fusion
  478.2 3.1 collective-permute-start.3
  482.7 1.9 constant_dynamic-update-slice_fusion.1
  484.7 63.5 %collective-permute-done.3 = bf16[128,4096]{1,0:T(8,128)(2,1)S(1)} collective-permute-done((bf16[128,4096]{1,0:T(8,128)(2,1)S(1)}, bf16[128,4096]{1,0:T(8,128)(2,1)S(1)}, u32[]{:S(2)}, u32[]{:S(2)}) %collective-permute-start.3) | collective-permute-done | bytes 1048608 | tf_op jit(solution)/shard_map/ppermute | solution.py:111
  548.2 1.2 constant_dynamic-update-slice_fusion
  549.4 2.0 copy-done.15
  551.3 1.9 collective-permute-start.4
  553.5 6.8 %reshape.263 = bf16[8192,1,128]{2,1,0:T(2,128)(2,1)} reshape(bf16[32,2,16384]{2,1,0:T(2,128)(2,1)S(1)} %all-to-all-done.5) | data formatting | bytes 4194304
  560.4 2.5 copy.77
  562.8 2.9 copy.76
  566.0 33.2 %collective-permute-done.4 = bf16[256,4096]{1,0:T(8,128)(2,1)} collective-permute-done((bf16[256,4096]{1,0:T(8,128)(2,1)}, bf16[256,4096]{1,0:T(8,128)(2,1)}, u32[]{:S(2)}, u32[]{:S(2)}) %collective-permute-start.4) | collective-permute-done | bytes 2097184 | tf_op jit(solution)/shard_map/ppermute | solution.py:111
  599.2 3.1 constant_dynamic-update-slice_fusion.5
  602.3 3.4 fusion.328
  606.6 4.3 collective-permute-start.5
  612.2 2.4 collective-permute-start.6
  615.4 3.6 collective-permute-done.6
  619.0 3.2 collective-permute-start.7
  623.0 2.7 collective-permute-done.7
  625.8 2.3 collective-permute-start.8
  628.9 5.7 collective-permute-done.8
  634.6 1.9 collective-permute-start.9
  637.3 6.5 collective-permute-done.9
  643.8 3.1 collective-permute-start.10
  648.0 2.4 collective-permute-done.10
  650.4 2.1 collective-permute-start.11
  653.6 2.6 collective-permute-done.11
  656.3 8.9 %collective-permute-start.12 = (f32[264,256]{1,0:T(8,128)S(1)}, f32[264,256]{1,0:T(8,128)S(1)}, u32[]{:S(2)}, u32[]{:S(2)}) collective-permute-start(f32[264,256]{1,0:T(8,128)S(1)} %maximum_select_fusion.1), channel_id=1, source_target_pairs={{0,32},{32,0},{64,96},{96,64},{128,160},{160,128},{192,224},{224,1... | collective-permute-start | bytes 811016 | tf_op jit(solution)/shard_map/ppermute | solution.py:151
  (138 shorter events, 40.7 us)
Async XLA Ops:
  4.3 21.0 %all-to-all-start.4 = ((bf16[32,2,1024]{2,1,0:T(2,128)(2,1)}), bf16[32,2,1024]{2,1,0:T(2,128)(2,1)S(1)}, u32[]{:S(2)}, u32[]{:S(2)}) async-start(bf16[32,2,1024]{2,1,0:T(2,128)(2,1)} %reshape.258), calls=%async_computation.4 | async-start | bytes 262144 | tf_op jit(solution)/shard_map/all_to_all | solution.py:177
  25.4 13.8 %all-to-all-start.2 = ((bf16[32,2,1024]{2,1,0:T(2,128)(2,1)}), bf16[32,2,1024]{2,1,0:T(2,128)(2,1)S(1)}, u32[]{:S(2)}, u32[]{:S(2)}) async-start(bf16[32,2,1024]{2,1,0:T(2,128)(2,1)} %reshape.256), calls=%async_computation.2 | async-start | bytes 262144 | tf_op jit(solution)/shard_map/all_to_all | solution.py:178
  56.9 7.7 %copy-start = (bf16[1,128,8192]{2,1,0:T(8,128)(2,1)S(1)}, bf16[1,128,8192]{2,1,0:T(8,128)(2,1)}, u32[]{:S(2)}) copy-start(bf16[1,128,8192]{2,1,0:T(8,128)(2,1)} %param.10) | copy-start | bytes 6291460
  56.9 214.0 %all-to-all-start = ((bf16[32,512,256]{2,1,0:T(8,128)(2,1)}), bf16[32,512,256]{2,1,0:T(8,128)(2,1)}, u32[]{:S(2)}, u32[]{:S(2)}) async-start(bf16[32,512,256]{2,1,0:T(8,128)(2,1)} %stack.2), calls=%async_computation | async-start | bytes 16777216 | tf_op jit(solution)/shard_map/all_to_all | solution.py:10
  64.5 2.0 copy-start.14
  67.3 0.7 copy-start.6
  67.6 0.7 copy-start.8
  290.0 71.1 %all-to-all-start.1 = ((bf16[32,2,1024]{2,1,0:T(2,128)(2,1)}), bf16[32,2,1024]{2,1,0:T(2,128)(2,1)}, u32[]{:S(2)}, u32[]{:S(2)}) async-start(bf16[32,2,1024]{2,1,0:T(2,128)(2,1)} %reshape.260), calls=%async_computation.1 | async-start | bytes 262144 | tf_op jit(solution)/shard_map/all_to_all | solution.py:180
  362.8 0.7 copy-start.4
  363.6 4.1 copy-start.2
  363.6 4.1 copy-start.3
  370.3 3.6 copy-start.13
  387.7 10.6 %copy-start.10 = (f32[2,8,64,128]{3,1,2,0:T(8,128)}, f32[2,8,64,128]{3,1,2,0:T(8,128)S(1)}, u32[]{:S(2)}) copy-start(f32[2,8,64,128]{3,1,2,0:T(8,128)S(1)} %copy.111) | copy-start | bytes 1572868
  388.5 9.7 %collective-permute-start = (bf16[16,4096]{1,0:T(8,128)(2,1)S(1)}, bf16[16,4096]{1,0:T(8,128)(2,1)S(1)}, u32[]{:S(2)}, u32[]{:S(2)}) collective-permute-start(bf16[16,4096]{1,0:T(8,128)(2,1)S(1)} %get-tuple-element.12), channel_id=1, source_target_pairs={{0,16},{1,17},{2,18},{3,19},{4,20},{5,21},{6,22},{7,23},{8,24},{9,... | collective-permute-start | bytes 393224 | tf_op jit(solution)/shard_map/ppermute | solution.py:111
  398.3 14.3 %collective-permute-start.1 = (bf16[32,4096]{1,0:T(8,128)(2,1)S(1)}, bf16[32,4096]{1,0:T(8,128)(2,1)S(1)}, u32[]{:S(2)}, u32[]{:S(2)}) collective-permute-start(bf16[32,4096]{1,0:T(8,128)(2,1)S(1)} %pad_maximum_fusion.4), channel_id=1, source_target_pairs={{0,8},{1,9},{2,10},{3,11},{4,12},{5,13},{6,14},{7,15},{8,0},{9,1},... | collective-permute-start | bytes 786440 | tf_op jit(solution)/shard_map/ppermute | solution.py:111
  413.4 63.7 %collective-permute-start.2 = (bf16[64,4096]{1,0:T(8,128)(2,1)}, bf16[64,4096]{1,0:T(8,128)(2,1)}, u32[]{:S(2)}, u32[]{:S(2)}) collective-permute-start(bf16[64,4096]{1,0:T(8,128)(2,1)} %pad_maximum_fusion.1), channel_id=1, source_target_pairs={{0,2},{1,3},{2,0},{3,1},{4,6},{5,7},{6,4},{7,5},{8,10},{9,11},{10,... | collective-permute-start | bytes 1572872 | tf_op jit(solution)/shard_map/ppermute | solution.py:111
  471.0 82.6 %all-to-all-start.5 = ((bf16[32,2,16384]{2,1,0:T(2,128)(2,1)}), bf16[32,2,16384]{2,1,0:T(2,128)(2,1)S(1)}, u32[]{:S(2)}, u32[]{:S(2)}) async-start(bf16[32,2,16384]{2,1,0:T(2,128)(2,1)} %reshape.262), calls=%async_computation.5 | async-start | bytes 4194304 | tf_op jit(solution)/shard_map/all_to_all | solution.py:165
  478.2 70.0 %collective-permute-start.3 = (bf16[128,4096]{1,0:T(8,128)(2,1)S(1)}, bf16[128,4096]{1,0:T(8,128)(2,1)S(1)}, u32[]{:S(2)}, u32[]{:S(2)}) collective-permute-start(bf16[128,4096]{1,0:T(8,128)(2,1)S(1)} %pad_maximum_fusion), channel_id=1, source_target_pairs={{0,4},{1,5},{2,6},{3,7},{4,0},{5,1},{6,2},{7,3},{8,12},{9,13},{10,... | collective-permute-start | bytes 3145736 | tf_op jit(solution)/shard_map/ppermute | solution.py:111
  549.4 2.0 copy-start.15
  551.3 47.9 %collective-permute-start.4 = (bf16[256,4096]{1,0:T(8,128)(2,1)}, bf16[256,4096]{1,0:T(8,128)(2,1)}, u32[]{:S(2)}, u32[]{:S(2)}) collective-permute-start(bf16[256,4096]{1,0:T(8,128)(2,1)} %get-tuple-element.19), channel_id=1, source_target_pairs={{0,1},{1,0},{2,3},{3,2},{4,5},{5,4},{6,7},{7,6},{8,9},{9,8},{10,11... | collective-permute-start | bytes 6291464 | tf_op jit(solution)/shard_map/ppermute | solution.py:111
  565.8 36.5 %copy-start.12 = (bf16[1,32,128,256]{3,2,1,0:T(8,128)(2,1)S(1)}, bf16[1,32,128,256]{3,2,1,0:T(8,128)(2,1)}, u32[]{:S(2)}) copy-start(bf16[1,32,128,256]{3,2,1,0:T(8,128)(2,1)} %copy.76) | copy-start | bytes 6291460
  605.8 8.8 %copy-start.1 = (f32[16,64,128]{2,1,0:T(8,128)S(1)}, f32[16,64,128]{2,1,0:T(8,128)}, u32[]{:S(2)}) copy-start(f32[16,64,128]{2,1,0:T(8,128)} %get-tuple-element.14) | copy-start | bytes 1572868
  606.6 5.4 collective-permute-start.5
  612.2 6.8 %collective-permute-start.6 = (f32[132,256]{1,0:T(8,128)S(1)}, f32[132,256]{1,0:T(8,128)S(1)}, u32[]{:S(2)}, u32[]{:S(2)}) collective-permute-start(f32[132,256]{1,0:T(8,128)S(1)} %slice_select_fusion.1), channel_id=1, source_target_pairs={{0,128},{32,160},{64,192},{96,224},{128,0},{160,32},{192,64},{224,... | collective-permute-start | bytes 405512 | tf_op jit(solution)/shard_map/ppermute | solution.py:149
  619.0 33.6 %copy-start.7 = (f32[1,32,128,16]{2,1,3,0:T(8,128)S(1)}, f32[1,32,128,16]{2,1,3,0:T(8,128)}, u32[]{:S(2)}) copy-start(f32[1,32,128,16]{2,1,3,0:T(8,128)} %copy-done.6) | copy-start | bytes 786436
  619.0 33.6 %copy-start.9 = (f32[1,32,128,16]{2,1,3,0:T(8,128)S(1)}, f32[1,32,128,16]{2,1,3,0:T(8,128)}, u32[]{:S(2)}) copy-start(f32[1,32,128,16]{2,1,3,0:T(8,128)} %copy-done.8) | copy-start | bytes 786436
  619.0 6.7 %collective-permute-start.7 = (f32[66,256]{1,0:T(8,128)S(1)}, f32[66,256]{1,0:T(8,128)S(1)}, u32[]{:S(2)}, u32[]{:S(2)}) collective-permute-start(f32[66,256]{1,0:T(8,128)S(1)} %slice_select_fusion.2), channel_id=1, source_target_pairs={{0,256},{32,288},{64,320},{96,352},{128,384},{160,416},{192,448},{... | collective-permute-start | bytes 202760 | tf_op jit(solution)/shard_map/ppermute | solution.py:149
  625.8 39.4 %copy-start.5 = (f32[1,32,128,16]{2,1,3,0:T(8,128)S(1)}, f32[1,32,128,16]{2,1,3,0:T(8,128)}, u32[]{:S(2)}) copy-start(f32[1,32,128,16]{2,1,3,0:T(8,128)} %copy-done.4) | copy-start | bytes 786436
  625.8 39.4 %copy-start.11 = (f32[2,8,64,128]{3,1,2,0:T(8,128)S(1)}, f32[2,8,64,128]{3,1,2,0:T(8,128)}, u32[]{:S(2)}) copy-start(f32[2,8,64,128]{3,1,2,0:T(8,128)} %copy-done.10) | copy-start | bytes 1572868
  625.8 8.8 %collective-permute-start.8 = (f32[33,256]{1,0:T(8,128)S(1)}, f32[33,256]{1,0:T(8,128)S(1)}, u32[]{:S(2)}, u32[]{:S(2)}) collective-permute-start(f32[33,256]{1,0:T(8,128)S(1)} %slice_select_fusion.3), channel_id=1, source_target_pairs={{0,64},{32,96},{64,0},{96,32},{128,192},{160,224},{192,128},{224,1... | collective-permute-start | bytes 101384 | tf_op jit(solution)/shard_map/ppermute | solution.py:149
  634.6 9.2 %collective-permute-start.9 = (f32[33,256]{1,0:T(8,128)S(1)}, f32[33,256]{1,0:T(8,128)S(1)}, u32[]{:S(2)}, u32[]{:S(2)}) collective-permute-start(f32[33,256]{1,0:T(8,128)S(1)} %select_add_fusion.3), channel_id=1, source_target_pairs={{0,64},{32,96},{64,0},{96,32},{128,192},{160,224},{192,128},{224,1... | collective-permute-start | bytes 101384 | tf_op jit(solution)/shard_map/ppermute | solution.py:151
  643.8 6.6 collective-permute-start.10
  650.4 5.8 collective-permute-start.11
  656.3 10.1 %collective-permute-start.12 = (f32[264,256]{1,0:T(8,128)S(1)}, f32[264,256]{1,0:T(8,128)S(1)}, u32[]{:S(2)}, u32[]{:S(2)}) collective-permute-start(f32[264,256]{1,0:T(8,128)S(1)} %maximum_select_fusion.1), channel_id=1, source_target_pairs={{0,32},{32,0},{64,96},{96,64},{128,160},{160,128},{192,224},{224,1... | collective-permute-start | bytes 811016 | tf_op jit(solution)/shard_map/ppermute | solution.py:151
